TPU v7x, 128 devices: a whole 4x4x4 slice. The times are simulated.
128 devices in a mesh: band: 4 (over x), pair: 32 (over z, y, core).
Axes of the slice: x: 4, y: 4, z: 4, core: 2. Of those that a mesh axis runs over, the one named last changes fastest.
Arguments:
- traces: float32 [16, 8192, 1024], P('band', 'pair'), may hold values from -300 to 300
- pair_list: int32 [256, 2], replicated, may hold values from 0 to 63, as said below
- pair_owner: int32 [256], replicated, may hold values from 0 to 63, as said below
Outputs:
- cross_spectra: bfloat16 [64, 2, 128, 128, 512], P('pair', None, None, None, 'band')
Inputs may be any that keep to these rules, and one draw needn't show every extreme that they name: `pair_list`: each row (i, j) has 8 <= j - i <= 24; index p of pair holds blocks p * 64 / 32 up to (p + 1) * 64 / 32 - 1, and the 16 blocks named by the rows of one owner (pair_owner // 2) all lie on different indices of pair. `pair_owner`: every slot is named by exactly 4 rows.
All inputs are finite; a program needn't handle non-finite values.
Results may differ from a plain program's by a relative error of at most 0.0057.
Values may be sent and summed in bfloat16 or wider, within the bound.
No kernel may reach another device: no remote copies, remote signals or barrier semaphores. Data moves between devices by JAX's collectives and lax.ppermute only.
A program may use at most 320 MiB of HBM per device.

v0:
```python
import jax
import jax.numpy as jnp
from jax import lax
from jax.sharding import PartitionSpec as P

SUB = 64
BLOCK = 128
SLOTS = 2
CHUNKS = 4


whiten_eps = 1e-05


def dft_table(samples, bins):
    bin_ids = jnp.broadcast_to(bins[:, None], (bins.shape[0], samples))
    sample_ids = lax.broadcasted_iota(jnp.int32, (bins.shape[0], samples), 1)
    phase_angle = (sample_ids * bin_ids % samples).astype(jnp.float32) * (2.0 * jnp.pi / samples)
    return jnp.concatenate([jnp.cos(phase_angle), -jnp.sin(phase_angle)], axis=0)


def whiten(flat_traces, bins):
    row_count, samples = flat_traces.shape
    bin_count = bins.shape[0]
    spectra = lax.dot_general(
        dft_table(samples, bins),
        flat_traces,
        (((1,), (1,)), ((), ())),
        precision=lax.Precision.HIGH,
        preferred_element_type=jnp.float32,
    )
    real_band = spectra[:bin_count].reshape(bin_count // SUB, SUB, row_count)
    imag_band = spectra[bin_count:].reshape(bin_count // SUB, SUB, row_count)
    band_power = jnp.mean(real_band * real_band + imag_band * imag_band, axis=1, keepdims=True)
    factor = lax.rsqrt(band_power + whiten_eps)
    stacked = jnp.stack([real_band * factor, imag_band * factor], axis=0)
    return stacked.reshape(2, bin_count, row_count).astype(jnp.bfloat16)


def slot_blocks(pair_list, pair_owner, slot_ids, per_slot):
    slot_match = (pair_owner[:, None] == slot_ids[None, :]).astype(jnp.int32)
    slot_rank = jnp.cumsum(slot_match, axis=0) - 1
    rank_ids = jnp.arange(per_slot, dtype=jnp.int32)
    selected = slot_match[:, :, None] * (slot_rank[:, :, None] == rank_ids[None, None, :]).astype(jnp.int32)
    first = jnp.sum(selected * pair_list[:, 0][:, None, None], axis=0)
    second = jnp.sum(selected * pair_list[:, 1][:, None, None], axis=0)
    return first, second


def shards(traces, pair_list, pair_owner):
    win_local, chan_local, samples = traces.shape
    bin_count = samples // 2
    bands = lax.axis_size("band")
    owners = lax.axis_size("pair")
    band_bins = bin_count // bands
    per_device = chan_local // BLOCK
    per_slot = pair_list.shape[0] // (owners * SLOTS)
    chunk = band_bins // CHUNKS

    flat = traces.reshape(win_local * chan_local, samples)
    halves = 2
    half_bins = band_bins // halves
    per_half = CHUNKS // halves
    pieces = []
    for half in range(halves):
        ids = jnp.arange(bands * half_bins, dtype=jnp.int32)
        bins = (ids // half_bins) * band_bins + half * half_bins + ids % half_bins
        whitened = whiten(flat, bins)
        whitened = whitened.reshape(2, bands, half_bins, win_local, per_device, BLOCK)
        whitened = jnp.transpose(whitened, (1, 4, 0, 3, 2, 5))
        for part in range(per_half):
            pieces.append(
                lax.all_to_all(
                    whitened[:, :, :, :, part * chunk:(part + 1) * chunk, :],
                    "band", split_axis=0, concat_axis=0, tiled=True,
                )
            )

    device_index = lax.axis_index("pair")
    slot_ids = device_index * SLOTS + jnp.arange(SLOTS, dtype=jnp.int32)
    first, second = slot_blocks(pair_list, pair_owner, slot_ids, per_slot)

    wanted = jnp.concatenate([first.reshape(-1), second.reshape(-1)])
    picks = (wanted[:, None] == jnp.arange(owners * per_device, dtype=jnp.int32)[None, :]).astype(jnp.bfloat16)
    products = []
    for part in range(CHUNKS):
        piece = jnp.transpose(pieces[part], (1, 0, 2, 3, 4, 5))
        gathered = lax.all_gather(piece, "pair", axis=0, tiled=True)
        if part == CHUNKS - 1 and part >= 1:
            gathered, products[-1] = lax.optimization_barrier((gathered, products[-1]))
        rows = gathered.shape[0]
        chosen = jnp.dot(picks, gathered.reshape(rows, -1), preferred_element_type=jnp.bfloat16)
        chosen = chosen.reshape(2, SLOTS, per_slot, *gathered.shape[1:])
        left = chosen[0]
        right = chosen[1]
        rotated = jnp.stack([-right[:, :, :, 1], right[:, :, :, 0]], axis=3)
        paired = jnp.stack([right, rotated], axis=1)
        product = jnp.einsum(
            "stgkwfa,sptgkwfb->spabf", left, paired, preferred_element_type=jnp.float32
        )
        product = product.astype(jnp.bfloat16)
        if part + 2 < CHUNKS:
            pieces[part + 2], product = lax.optimization_barrier((pieces[part + 2], product))
        products.append(product)
    out = jnp.zeros((SLOTS, 2, BLOCK, BLOCK, band_bins), jnp.bfloat16)
    for part in range(CHUNKS):
        out = lax.dynamic_update_slice_in_dim(out, products[part], part * chunk, axis=4)
    return out


def solution(mesh):
    placed = (P("band", "pair", None), P(), P())
    return jax.shard_map(
        shards,
        mesh=mesh,
        in_specs=placed,
        out_specs=P("pair", None, None, None, "band"),
        check_vma=False,
    )
```

profile of v0, /device:TPU:1, one launch (start us, length us, event | category | flops | bytes accessed | tf_op | source)
XLA Modules:
  0.0 392.8 jit_solution(14218724183505803486)
XLA Ops:
  6.5 4.2 %fusion.69 = (f32[256,1024]{1,0:T(8,128)S(1)}, f32[256,1024]{1,0:T(8,128)S(1)}) fusion(s32[256]{0:T(256)S(1)} %get-tuple-element.50), kind=kLoop, calls=%fused_computation.99 | loop fusion | flops 3932160 | bytes 2098176 | tf_op jit(solution)/shard_map/cos | solution.py:19
  10.8 5.7 %fusion.45 = f32[512,1024]{1,0:T(8,128)S(1)} fusion(f32[1024,1024]{1,0:T(8,128)} %bitcast.173, f32[256,1024]{1,0:T(8,128)S(1)} %get-tuple-element.46, f32[256,1024]{1,0:T(8,128)S(1)} %get-tuple-element.45), kind=kOutput, calls=%fused_computation.49 | convolution fusion | flops 3221749760 | bytes 8388608 | tf_op jit(solution)/shard_map/dot_general | solution.py:25
  18.3 13.3 %all_to_all.20 = bf16[4,2,2,4,32,128]{5,4,3,2,1,0:T(8,128)(2,1)S(1)} all-to-all(bf16[4,2,2,4,32,128]{5,4,3,2,1,0:T(8,128)(2,1)S(1)} %get-tuple-element.40), channel_id=1, replica_groups=mesh['band'=4,'pair'=32] {'band'}, dimensions={0} | all-to-all | bytes 1048576 | tf_op jit(solution)/shard_map/all_to_all | solution.py:73
  32.4 10.3 %all_to_all.21 = bf16[4,2,2,4,32,128]{5,4,3,2,1,0:T(8,128)(2,1)S(1)} all-to-all(bf16[4,2,2,4,32,128]{5,4,3,2,1,0:T(8,128)(2,1)S(1)} %get-tuple-element.39), channel_id=1, replica_groups=mesh['band'=4,'pair'=32] {'band'}, dimensions={0} | all-to-all | bytes 1048576 | tf_op jit(solution)/shard_map/all_to_all | solution.py:73
  43.6 4.2 %fusion.70 = (f32[256,1024]{1,0:T(8,128)S(1)}, f32[256,1024]{1,0:T(8,128)S(1)}) fusion(s32[256]{0:T(256)S(1)} %get-tuple-element.49), kind=kLoop, calls=%fused_computation.100 | loop fusion | flops 3932160 | bytes 2098176 | tf_op jit(solution)/shard_map/cos | solution.py:19
  47.8 5.7 %fusion.41 = f32[512,1024]{1,0:T(8,128)S(1)} fusion(f32[1024,1024]{1,0:T(8,128)} %bitcast.174, f32[256,1024]{1,0:T(8,128)S(1)} %get-tuple-element.48, f32[256,1024]{1,0:T(8,128)S(1)} %get-tuple-element.47), kind=kOutput, calls=%fused_computation.45 | convolution fusion | flops 3221749760 | bytes 8388608 | tf_op jit(solution)/shard_map/dot_general | solution.py:25
  56.3 3.5 all-to-all-start
  61.9 45.4 %all-gather.5.cloned.1.call-done = bf16[64,4,2,4,32,128]{5,4,3,2,1,0:T(8,128)(2,1)} async-done(((bf16[2,4,2,4,32,128]{5,4,3,2,1,0:T(8,128)(2,1)}), bf16[64,4,2,4,32,128]{5,4,3,2,1,0:T(8,128)(2,1)}) %all-gather.5.cloned.1.call-update) | async-done | bytes 16777232 | tf_op jit(solution)/shard_map/all_gather | solution.py:88
  107.3 14.9 %fusion.9 = bf16[16,131072]{1,0:T(8,128)(2,1)S(1)} fusion(bf16[8,8,1024,128]{3,2,1,0:T(8,128)(2,1)} %bitcast.170, s32[16]{0:T(128)S(1)} %pad_add_fusion), kind=kOutput, calls=%fused_computation.9 | convolution fusion | flops 268436480 | bytes 20971584 | tf_op jit(solution)/shard_map/dot_general | solution.py:92
  127.3 6.2 %fusion.12 = bf16[2,2,128,128,32]{2,3,1,4,0:T(8,128)(2,1)} fusion(bf16[2,1,4,4,2,4,32,128]{7,5,2,4,3,1,6,0:T(4,128)(2,1)S(1)} %maximum_bitcast_fusion, bf16[2,1,4,4,2,4,32,128]{7,5,2,4,3,1,6,0:T(4,128)(2,1)S(1)} %copy.77, bf16[2,4,4,2,4,32,128,1]{6,5,4,3,2,1,0,7:T(8,128)(2,1)S(1)} %bitcast.176), kind=kOutput, calls=%fused_computation.16 | convolution fusion | flops 547356672 | bytes 10485760 | tf_op jit(solution)/shard_map/stgkwfa,sptgkwfb->spabf/dot_general | solution.py:98
  134.4 4.0 %all-to-all-start.2 = ((bf16[4,2,2,4,32,128]{5,4,3,2,1,0:T(8,128)(2,1)}), bf16[4,2,2,4,32,128]{5,4,3,2,1,0:T(8,128)(2,1)S(1)}, u32[]{:S(2)}, u32[]{:S(2)}) async-start(bf16[4,2,2,4,32,128]{5,4,3,2,1,0:T(8,128)(2,1)} %get-tuple-element.41), calls=%async_computation.2 | async-start | bytes 1048576 | tf_op jit(solution)/shard_map/all_to_all | solution.py:73
  138.4 43.3 %all-gather.7.cloned.1.call-done = bf16[64,4,2,4,32,128]{5,4,3,2,1,0:T(8,128)(2,1)} async-done(((bf16[2,4,2,4,32,128]{5,4,3,2,1,0:T(8,128)(2,1)}), bf16[64,4,2,4,32,128]{5,4,3,2,1,0:T(8,128)(2,1)}) %all-gather.7.cloned.1.call-update) | async-done | bytes 16777232 | tf_op jit(solution)/shard_map/all_gather | solution.py:88
  181.6 14.9 %fusion.6 = bf16[16,131072]{1,0:T(8,128)(2,1)S(1)} fusion(bf16[8,8,1024,128]{3,2,1,0:T(8,128)(2,1)} %bitcast.169, s32[16]{0:T(128)S(1)} %pad_add_fusion), kind=kOutput, calls=%fused_computation.6 | convolution fusion | flops 268436480 | bytes 20971584 | tf_op jit(solution)/shard_map/dot_general | solution.py:92
  201.9 6.3 %fusion.13 = bf16[2,2,128,128,32]{2,3,1,4,0:T(8,128)(2,1)} fusion(bf16[2,1,4,4,2,4,32,128]{7,5,2,4,3,1,6,0:T(4,128)(2,1)S(1)} %maximum_bitcast_fusion.1, bf16[2,1,4,4,2,4,32,128]{7,5,2,4,3,1,6,0:T(4,128)(2,1)S(1)} %copy.82, bf16[2,4,4,2,4,32,128,1]{6,5,4,3,2,1,0,7:T(8,128)(2,1)S(1)} %bitcast.177), kind=kOutput, calls=%fused_computation.17 | convolution fusion | flops 547356672 | bytes 10485760 | tf_op jit(solution)/shard_map/stgkwfa,sptgkwfb->spabf/dot_general | solution.py:98
  209.1 9.0 %dynamic_update_slice.12 = bf16[2,2,128,128,128]{2,3,1,4,0:T(8,128)(2,1)} pad(bf16[2,2,128,128,32]{2,3,1,4,0:T(8,128)(2,1)} %fusion.12, bf16[]{:T(256)} %constant.86.clone.1), padding=0_0x0_0x0_0x0_0x0_96 | pad | bytes 20971522 | tf_op jit(solution)/shard_map/dynamic_update_slice | solution.py:107
  218.1 2.9 constant_dynamic-update-slice_fusion.1
  221.0 35.1 %all-gather.11.cloned.1.call-done = bf16[64,4,2,4,32,128]{5,4,3,2,1,0:T(8,128)(2,1)} async-done(((bf16[2,4,2,4,32,128]{5,4,3,2,1,0:T(8,128)(2,1)}), bf16[64,4,2,4,32,128]{5,4,3,2,1,0:T(8,128)(2,1)}) %all-gather.11.cloned.1.call-update) | async-done | bytes 16777232 | tf_op jit(solution)/shard_map/all_gather | solution.py:88
  256.0 14.9 %fusion.3 = bf16[16,131072]{1,0:T(8,128)(2,1)S(1)} fusion(bf16[8,8,1024,128]{3,2,1,0:T(8,128)(2,1)} %bitcast.171, s32[16]{0:T(128)S(1)} %pad_add_fusion), kind=kOutput, calls=%fused_computation.3 | convolution fusion | flops 268436480 | bytes 20971584 | tf_op jit(solution)/shard_map/dot_general | solution.py:92
  276.1 6.2 %fusion.14 = bf16[2,2,128,128,32]{2,3,1,4,0:T(8,128)(2,1)} fusion(bf16[2,1,4,4,2,4,32,128]{7,5,2,4,3,1,6,0:T(4,128)(2,1)S(1)} %maximum_bitcast_fusion.2, bf16[2,1,4,4,2,4,32,128]{7,5,2,4,3,1,6,0:T(4,128)(2,1)S(1)} %copy.88, bf16[2,4,4,2,4,32,128,1]{6,5,4,3,2,1,0,7:T(8,128)(2,1)S(1)} %bitcast.178), kind=kOutput, calls=%fused_computation.18 | convolution fusion | flops 547356672 | bytes 10485760 | tf_op jit(solution)/shard_map/stgkwfa,sptgkwfb->spabf/dot_general | solution.py:98
  282.3 48.0 %all-gather.9.cloned.1.call-done = bf16[64,4,2,4,32,128]{5,4,3,2,1,0:T(8,128)(2,1)} async-done(((bf16[2,4,2,4,32,128]{5,4,3,2,1,0:T(8,128)(2,1)}), bf16[64,4,2,4,32,128]{5,4,3,2,1,0:T(8,128)(2,1)}) %all-gather.9.cloned.1.call-update) | async-done | bytes 16777232 | tf_op jit(solution)/shard_map/all_gather | solution.py:88
  330.3 14.9 %fusion = bf16[16,131072]{1,0:T(8,128)(2,1)S(1)} fusion(bf16[8,8,1024,128]{3,2,1,0:T(8,128)(2,1)} %bitcast.172, s32[16]{0:T(128)S(1)} %pad_add_fusion), kind=kOutput, calls=%fused_computation | convolution fusion | flops 268436480 | bytes 20971584 | tf_op jit(solution)/shard_map/dot_general | solution.py:92
  351.2 2.8 constant_dynamic-update-slice_fusion
  354.0 6.2 %fusion.16 = bf16[2,2,128,128,128]{2,3,1,4,0:T(8,128)(2,1)} fusion(bf16[2,2,128,128,128]{2,3,1,4,0:T(8,128)(2,1)} %constant_dynamic-update-slice_fusion, bf16[2,1,4,4,2,4,32,128]{7,5,2,4,3,1,6,0:T(4,128)(2,1)S(1)} %maximum_bitcast_fusion.3, bf16[2,1,4,4,2,4,32,128]{7,5,2,4,3,1,6,0:T(4,128)(2,1)S(1)} %copy.92, ...), kind=kOutput, calls=%fused_computation.20 | convolution fusion | flops 547356672 | bytes 10485760 | tf_op jit(solution)/shard_map/stgkwfa,sptgkwfb->spabf/dot_general | solution.py:98
  360.2 25.8 %copy.94 = bf16[2,2,128,128,128]{4,3,2,1,0:T(8,128)(2,1)} copy(bf16[2,2,128,128,128]{2,3,1,4,0:T(8,128)(2,1)} %fusion.16) | data formatting | bytes 33554432 | tf_op jit(solution)/shard_map/dynamic_update_slice | solution.py:107
  (86 shorter events, 31.3 us)
Async XLA Ops:
  6.5 100.7 %all-gather.5.cloned.1.call-start = ((), (), s32[]{:S(2)}) async-start(), calls=%async_computation.4 | async-start | bytes 17301504 | tf_op jit(solution)/shard_map/all_gather | solution.py:88
  32.4 149.3 %all-gather.7.cloned.1.call-start = ((), (), s32[]{:S(2)}) async-start(), calls=%async_computation.5 | async-start | bytes 17301504 | tf_op jit(solution)/shard_map/all_gather | solution.py:88
  55.2 4.7 %copy-start.2 = (s32[256]{0:T(256)S(1)}, s32[256]{0:T(256)}, u32[]{:S(2)}) copy-start(s32[256]{0:T(256)} %param.5) | copy-start | bytes 3076
  55.2 6.3 %copy-start.3 = (s32[256,2]{0,1:T(2,128)S(1)}, s32[256,2]{0,1:T(2,128)}, u32[]{:S(2)}) copy-start(s32[256,2]{0,1:T(2,128)} %param.4) | copy-start | bytes 6148
  56.3 77.2 %all-to-all-start = ((bf16[4,2,2,4,32,128]{5,4,3,2,1,0:T(8,128)(2,1)}), bf16[4,2,2,4,32,128]{5,4,3,2,1,0:T(8,128)(2,1)S(1)}, u32[]{:S(2)}, u32[]{:S(2)}) async-start(bf16[4,2,2,4,32,128]{5,4,3,2,1,0:T(8,128)(2,1)} %get-tuple-element.42), calls=%async_computation | async-start | bytes 1048576 | tf_op jit(solution)/shard_map/all_to_all | solution.py:73
  59.8 196.2 %all-gather.11.cloned.1.call-start = ((), (), s32[]{:S(2)}) async-start(), calls=%async_computation.7 | async-start | bytes 17301504 | tf_op jit(solution)/shard_map/all_gather | solution.py:88
  134.4 73.8 %all-to-all-start.2 = ((bf16[4,2,2,4,32,128]{5,4,3,2,1,0:T(8,128)(2,1)}), bf16[4,2,2,4,32,128]{5,4,3,2,1,0:T(8,128)(2,1)S(1)}, u32[]{:S(2)}, u32[]{:S(2)}) async-start(bf16[4,2,2,4,32,128]{5,4,3,2,1,0:T(8,128)(2,1)} %get-tuple-element.41), calls=%async_computation.2 | async-start | bytes 1048576 | tf_op jit(solution)/shard_map/all_to_all | solution.py:73
  138.4 191.9 %all-gather.9.cloned.1.call-start = ((), (), s32[]{:S(2)}) async-start(), calls=%async_computation.6 | async-start | bytes 17301504 | tf_op jit(solution)/shard_map/all_gather | solution.py:88
  209.1 9.0 %copy-start.1 = (bf16[2,2,128,128,32]{2,3,1,4,0:T(8,128)(2,1)S(1)}, bf16[2,2,128,128,32]{2,3,1,4,0:T(8,128)(2,1)}, u32[]{:S(2)}) copy-start(bf16[2,2,128,128,32]{2,3,1,4,0:T(8,128)(2,1)} %fusion.13) | copy-start | bytes 12582916
  349.0 2.2 copy-start
Sparse Core Ops, SparseCore 0:
  32.5 74.7 all-gather.4
  109.5 72.0 all-gather.6
  183.9 72.0 all-gather.10
  258.1 72.0 all-gather.8
where the time goes:
time: 400 us; the launch traced here: 393 us
  waiting for transfers between devices  172 us (43%)
  matrix products  96 us (24%)
  local copies, waits for them, and re-layouts  60.7 us (15%)
  blocking collectives  23.6 us (6%)
  other arithmetic  19.4 us (5%)
  between operations  13.8 us (3%)
  starting transfers between devices  7.54 us (2%)
    all_gather x4, waiting for transfers between devices, shards(): gathered = lax.all_gather(piece, 'pair', axis=0, tiled=True)  172 us
    dot_general x4, matrix products, shards(): jnp.dot(picks, gathered.reshape(rows, -1), preferred_element_type=jnp.bfl...  59.6 us
    dynamic_update_slice x4, local copies, waits for them, and re-layouts, shards(): lax.dynamic_update_slice_in_dim(out, products[part], part * chunk, axis=4)  40.5 us
    dot_general x4, matrix products, shards(): jnp.einsum('stgkwfa,sptgkwfb->spabf', left, paired, preferred_element_typ...  24.9 us
    all_to_all x2, blocking collectives, shards(): lax.all_to_all(whitened[:, :, :, :, part * chunk:(part + 1) * chunk, :],...  23.6 us
    dot_general x2, matrix products, whiten(): lax.dot_general(dft_table(samples, bins), flat_traces, (((1,), (1,)), (()...  11.4 us
    cos x2, other arithmetic, dft_table(): jnp.cos(phase_angle)  8.41 us
  transfers between devices with their start and end apart: 6, of which 4 were waited for; matrix products, arithmetic and copies ran while one was open for 27% of the time, Pallas kernels for 0%

commit v1 on v0

--- a/solution.py
+++ b/solution.py
@@ -6,7 +6,6 @@
 SUB = 64
 BLOCK = 128
 SLOTS = 2
-CHUNKS = 4
 
 
 whiten_eps = 1e-05
@@ -55,26 +54,29 @@
     band_bins = bin_count // bands
     per_device = chan_local // BLOCK
     per_slot = pair_list.shape[0] // (owners * SLOTS)
-    chunk = band_bins // CHUNKS
 
     flat = traces.reshape(win_local * chan_local, samples)
     halves = 2
     half_bins = band_bins // halves
-    per_half = CHUNKS // halves
-    pieces = []
+    edges = [0, 3 * band_bins // 8, 6 * band_bins // 8, band_bins]
+    spans = []
     for half in range(halves):
         ids = jnp.arange(bands * half_bins, dtype=jnp.int32)
         bins = (ids // half_bins) * band_bins + half * half_bins + ids % half_bins
         whitened = whiten(flat, bins)
         whitened = whitened.reshape(2, bands, half_bins, win_local, per_device, BLOCK)
-        whitened = jnp.transpose(whitened, (1, 4, 0, 3, 2, 5))
-        for part in range(per_half):
-            pieces.append(
-                lax.all_to_all(
-                    whitened[:, :, :, :, part * chunk:(part + 1) * chunk, :],
-                    "band", split_axis=0, concat_axis=0, tiled=True,
-                )
-            )
+        spans.append(jnp.transpose(whitened, (1, 4, 0, 3, 2, 5)))
+    pieces = []
+    for low, high in zip(edges[:-1], edges[1:]):
+        parts = []
+        for half in range(halves):
+            start = max(low, half * half_bins)
+            stop = min(high, (half + 1) * half_bins)
+            if start < stop:
+                parts.append(spans[half][:, :, :, :, start - half * half_bins:stop - half * half_bins, :])
+        chunk_bins = parts[0] if len(parts) == 1 else jnp.concatenate(parts, axis=4)
+        pieces.append(lax.all_to_all(chunk_bins, "band", split_axis=0, concat_axis=0, tiled=True))
+    chunks = len(pieces)
 
     device_index = lax.axis_index("pair")
     slot_ids = device_index * SLOTS + jnp.arange(SLOTS, dtype=jnp.int32)
@@ -83,10 +85,10 @@
     wanted = jnp.concatenate([first.reshape(-1), second.reshape(-1)])
     picks = (wanted[:, None] == jnp.arange(owners * per_device, dtype=jnp.int32)[None, :]).astype(jnp.bfloat16)
     products = []
-    for part in range(CHUNKS):
+    for part in range(chunks):
         piece = jnp.transpose(pieces[part], (1, 0, 2, 3, 4, 5))
         gathered = lax.all_gather(piece, "pair", axis=0, tiled=True)
-        if part == CHUNKS - 1 and part >= 1:
+        if part == chunks - 1 and part >= 1:
             gathered, products[-1] = lax.optimization_barrier((gathered, products[-1]))
         rows = gathered.shape[0]
         chosen = jnp.dot(picks, gathered.reshape(rows, -1), preferred_element_type=jnp.bfloat16)
@@ -99,12 +101,12 @@
             "stgkwfa,sptgkwfb->spabf", left, paired, preferred_element_type=jnp.float32
         )
         product = product.astype(jnp.bfloat16)
-        if part + 2 < CHUNKS:
+        if part + 2 < chunks:
             pieces[part + 2], product = lax.optimization_barrier((pieces[part + 2], product))
         products.append(product)
     out = jnp.zeros((SLOTS, 2, BLOCK, BLOCK, band_bins), jnp.bfloat16)
-    for part in range(CHUNKS):
-        out = lax.dynamic_update_slice_in_dim(out, products[part], part * chunk, axis=4)
+    for part in range(chunks):
+        out = lax.dynamic_update_slice_in_dim(out, products[part], edges[part], axis=4)
     return out
 
 

time: 400 us -> 405 us (1.012)
  matrix products: 96 us -> 215 us
  waiting for transfers between devices: 172 us -> 61.7 us
  blocking collectives: 23.6 us -> 29 us
  local copies, waits for them, and re-layouts: 60.7 us -> 55.7 us
    dot_general x4 -> x3, matrix products: 59.6 us -> 180 us  [shards(): jnp.dot(picks, gathered.reshape(rows, -1), preferred_element_type=jnp.bfl...]
    all_gather x4 -> x3, waiting for transfers between devices: 172 us -> 61.6 us  [shards(): gathered = lax.all_gather(piece, 'pair', axis=0, tiled=True)]
    all_to_all x2, blocking collectives: 23.6 us -> 29 us  [shards(): lax.all_to_all(chunk_bins, 'band', split_axis=0, concat_axis=0, tiled=True)]
    dynamic_update_slice x4 -> x3, local copies, waits for them, and re-layouts: 40.5 us -> 36.3 us  [shards(): lax.dynamic_update_slice_in_dim(out, products[part], edges[part], axis=4)]
    dot_general x4 -> x3, matrix products: 24.9 us -> 23.6 us  [shards(): jnp.einsum('stgkwfa,sptgkwfb->spabf', left, paired, preferred_element_typ...]
  transfers between devices with their start and end apart: 6 -> 4, of which waited for: 4 -> 1; matrix products, arithmetic and copies ran while one was open for 27% -> 55% of each run, Pallas kernels for 0% -> 0%
where the time goes in v1:
time: 405 us; the launch traced here: 398 us
  matrix products  215 us (53%)
  waiting for transfers between devices  61.7 us (15%)
  local copies, waits for them, and re-layouts  55.7 us (14%)
  blocking collectives  29 us (7%)
  other arithmetic  18.9 us (5%)
  between operations  13.9 us (3%)
  starting transfers between devices  4.45 us (1%)
    dot_general x3, matrix products, shards(): jnp.dot(picks, gathered.reshape(rows, -1), preferred_element_type=jnp.bfl...  180 us
    all_gather x3, waiting for transfers between devices, shards(): gathered = lax.all_gather(piece, 'pair', axis=0, tiled=True)  61.6 us
    dynamic_update_slice x3, local copies, waits for them, and re-layouts, shards(): lax.dynamic_update_slice_in_dim(out, products[part], edges[part], axis=4)  36.3 us
    all_to_all x2, blocking collectives, shards(): lax.all_to_all(chunk_bins, 'band', split_axis=0, concat_axis=0, tiled=True)  29 us
    dot_general x3, matrix products, shards(): jnp.einsum('stgkwfa,sptgkwfb->spabf', left, paired, preferred_element_typ...  23.6 us
    dot_general x2, matrix products, whiten(): lax.dot_general(dft_table(samples, bins), flat_traces, (((1,), (1,)), (()...  11.4 us
    cos x2, other arithmetic, dft_table(): jnp.cos(phase_angle)  8.42 us
  transfers between devices with their start and end apart: 4, of which 1 were waited for; matrix products, arithmetic and copies ran while one was open for 55% of the time, Pallas kernels for 0%

profile of v1, /device:TPU:1, one launch (start us, length us, event | category | flops | bytes accessed | tf_op | source)
XLA Modules:
  0.0 398.3 jit_solution(2391721877628682663)
XLA Ops:
  6.5 4.2 %fusion.58 = (f32[256,1024]{1,0:T(8,128)S(1)}, f32[256,1024]{1,0:T(8,128)S(1)}) fusion(s32[256]{0:T(256)S(1)} %fusion.68), kind=kLoop, calls=%fused_computation.86 | loop fusion | flops 3932160 | bytes 2098176 | tf_op jit(solution)/shard_map/cos | solution.py:18
  10.8 5.7 %fusion.37 = f32[512,1024]{1,0:T(8,128)S(1)} fusion(f32[1024,1024]{1,0:T(8,128)} %bitcast.140, f32[256,1024]{1,0:T(8,128)S(1)} %get-tuple-element.36, f32[256,1024]{1,0:T(8,128)S(1)} %get-tuple-element.35), kind=kOutput, calls=%fused_computation.42 | convolution fusion | flops 3221749760 | bytes 8388608 | tf_op jit(solution)/shard_map/dot_general | solution.py:24
  18.2 16.1 %all_to_all.15 = bf16[4,2,2,4,48,128]{5,4,3,2,1,0:T(8,128)(2,1)S(1)} all-to-all(bf16[4,2,2,4,48,128]{5,4,3,2,1,0:T(8,128)(2,1)S(1)} %slice.108), channel_id=1, replica_groups=mesh['band'=4,'pair'=32] {'band'}, dimensions={0} | all-to-all | bytes 1572864 | tf_op jit(solution)/shard_map/all_to_all | solution.py:78
  35.5 4.2 %fusion.59 = (f32[256,1024]{1,0:T(8,128)S(1)}, f32[256,1024]{1,0:T(8,128)S(1)}) fusion(s32[256]{0:T(256)S(1)} %add_add_fusion), kind=kLoop, calls=%fused_computation.87 | loop fusion | flops 3932160 | bytes 2098176 | tf_op jit(solution)/shard_map/cos | solution.py:18
  39.7 5.7 %fusion.33 = f32[512,1024]{1,0:T(8,128)S(1)} fusion(f32[1024,1024]{1,0:T(8,128)} %bitcast.141, f32[256,1024]{1,0:T(8,128)S(1)} %get-tuple-element.38, f32[256,1024]{1,0:T(8,128)S(1)} %get-tuple-element.37), kind=kOutput, calls=%fused_computation.38 | convolution fusion | flops 3221749760 | bytes 8388608 | tf_op jit(solution)/shard_map/dot_general | solution.py:24
  48.1 13.0 %all_to_all.16 = bf16[4,2,2,4,48,128]{5,4,3,2,1,0:T(8,128)(2,1)S(1)} all-to-all(bf16[4,2,2,4,48,128]{5,4,3,2,1,0:T(8,128)(2,1)S(1)} %pad_maximum_fusion), channel_id=1, replica_groups=mesh['band'=4,'pair'=32] {'band'}, dimensions={0} | all-to-all | bytes 1572864 | tf_op jit(solution)/shard_map/all_to_all | solution.py:78
  62.0 4.2 %all-to-all-start = ((bf16[4,2,2,4,32,128]{5,4,3,2,1,0:T(8,128)(2,1)}), bf16[4,2,2,4,32,128]{5,4,3,2,1,0:T(8,128)(2,1)}, u32[]{:S(2)}, u32[]{:S(2)}) async-start(bf16[4,2,2,4,32,128]{5,4,3,2,1,0:T(8,128)(2,1)} %get-tuple-element.32), calls=%async_computation | async-start | bytes 1048576 | tf_op jit(solution)/shard_map/all_to_all | solution.py:78
  67.9 61.6 %all-gather.4.cloned.1.call-done = bf16[64,4,2,4,48,128]{5,4,3,2,1,0:T(8,128)(2,1)} async-done(((bf16[2,4,2,4,48,128]{5,4,3,2,1,0:T(8,128)(2,1)}), bf16[64,4,2,4,48,128]{5,4,3,2,1,0:T(8,128)(2,1)}) %all-gather.4.cloned.1.call-update) | async-done | bytes 25165840 | tf_op jit(solution)/shard_map/all_gather | solution.py:90
  129.5 82.3 %fusion.3 = bf16[16,196608]{1,0:T(8,128)(2,1)S(1)} fusion(bf16[8,8,1536,128]{3,2,1,0:T(8,128)(2,1)} %bitcast.135, s32[16]{0:T(128)S(1)} %pad_add_fusion), kind=kOutput, calls=%fused_computation.3 | convolution fusion | flops 402654208 | bytes 31457344 | tf_op jit(solution)/shard_map/dot_general | solution.py:94
  213.1 1.8 copy.64
  217.2 2.0 maximum_bitcast_fusion
  219.3 8.6 %fusion.9 = bf16[2,2,128,128,48]{2,3,1,4,0:T(8,128)(2,1)} fusion(bf16[2,1,4,4,2,4,48,128]{7,5,2,4,3,1,6,0:T(4,128)(2,1)S(1)} %maximum_bitcast_fusion, bf16[2,1,4,4,2,4,48,128]{7,5,2,4,3,1,6,0:T(4,128)(2,1)S(1)} %copy.64, bf16[2,4,4,2,4,48,128,1]{6,5,4,3,2,1,0,7:T(8,128)(2,1)S(1)} %bitcast.147), kind=kOutput, calls=%fused_computation.12 | convolution fusion | flops 821035008 | bytes 15728640 | tf_op jit(solution)/shard_map/stgkwfa,sptgkwfb->spabf/dot_general | solution.py:100
  227.9 1.9 copy.66
  229.8 82.5 %fusion = bf16[16,196608]{1,0:T(8,128)(2,1)S(1)} fusion(bf16[8,8,1536,128]{3,2,1,0:T(8,128)(2,1)} %bitcast.136, s32[16]{0:T(128)S(1)} %pad_add_fusion), kind=kOutput, calls=%fused_computation | convolution fusion | flops 402654208 | bytes 31457344 | tf_op jit(solution)/shard_map/dot_general | solution.py:94
  313.6 1.8 copy.70
  317.1 6.4 %dynamic_update_slice.9 = bf16[2,2,128,128,128]{2,3,1,4,0:T(8,128)(2,1)} pad(bf16[2,2,128,128,48]{2,3,1,4,0:T(8,128)(2,1)S(1)} %bitcast.145, bf16[]{:T(256)} %constant.86.clone.1), padding=0_0x0_0x0_0x0_0x0_80 | pad | bytes 23068674 | tf_op jit(solution)/shard_map/dynamic_update_slice | solution.py:109
  324.4 2.0 maximum_bitcast_fusion.1
  326.4 8.8 %fusion.10 = bf16[2,2,128,128,48]{2,3,1,4,0:T(8,128)(2,1)} fusion(bf16[2,1,4,4,2,4,48,128]{7,5,2,4,3,1,6,0:T(4,128)(2,1)S(1)} %maximum_bitcast_fusion.1, bf16[2,1,4,4,2,4,48,128]{7,5,2,4,3,1,6,0:T(4,128)(2,1)S(1)} %copy.70, bf16[2,4,4,2,4,48,128,1]{6,5,4,3,2,1,0,7:T(8,128)(2,1)S(1)} %bitcast.146), kind=kOutput, calls=%fused_computation.13 | convolution fusion | flops 821035008 | bytes 15728640 | tf_op jit(solution)/shard_map/stgkwfa,sptgkwfb->spabf/dot_general | solution.py:100
  335.2 14.9 %fusion.6 = bf16[16,131072]{1,0:T(8,128)(2,1)S(1)} fusion(bf16[8,8,1024,128]{3,2,1,0:T(8,128)(2,1)} %bitcast.139, s32[16]{0:T(128)S(1)} %pad_add_fusion), kind=kOutput, calls=%fused_computation.6 | convolution fusion | flops 268436480 | bytes 20971584 | tf_op jit(solution)/shard_map/dot_general | solution.py:94
  351.0 1.1 copy.74
  354.0 1.4 maximum_bitcast_fusion.2
  355.4 4.1 %constant_dynamic-update-slice_fusion = bf16[2,2,128,128,128]{2,3,1,4,0:T(8,128)(2,1)} fusion(bf16[2,2,128,128,128]{2,3,1,4,0:T(8,128)(2,1)} %dynamic_update_slice.9, bf16[2,2,128,128,48]{2,3,1,4,0:T(8,128)(2,1)S(1)} %bitcast.143), kind=kLoop, calls=%fused_computation.114 | loop fusion | bytes 12582912 | tf_op jit(solution)/shard_map/dynamic_update_slice | solution.py:109
  359.5 6.2 %fusion.20 = bf16[2,2,128,128,128]{2,3,1,4,0:T(8,128)(2,1)} fusion(bf16[2,2,128,128,128]{2,3,1,4,0:T(8,128)(2,1)} %constant_dynamic-update-slice_fusion, bf16[2,1,4,4,2,4,32,128]{7,5,2,4,3,1,6,0:T(4,128)(2,1)S(1)} %maximum_bitcast_fusion.2, bf16[2,1,4,4,2,4,32,128]{7,5,2,4,3,1,6,0:T(4,128)(2,1)S(1)} %copy.74, ...), kind=kOutput, calls=%fused_computation.23 | convolution fusion | flops 547356672 | bytes 10485760 | tf_op jit(solution)/shard_map/stgkwfa,sptgkwfb->spabf/dot_general | solution.py:100
  365.7 25.8 %copy.76 = bf16[2,2,128,128,128]{4,3,2,1,0:T(8,128)(2,1)} copy(bf16[2,2,128,128,128]{2,3,1,4,0:T(8,128)(2,1)} %fusion.20) | data formatting | bytes 33554432 | tf_op jit(solution)/shard_map/dynamic_update_slice | solution.py:109
  (81 shorter events, 18.2 us)
Async XLA Ops:
  6.5 123.0 %all-gather.4.cloned.1.call-start = ((), (), s32[]{:S(2)}) async-start(), calls=%async_computation.3 | async-start | bytes 25952256 | tf_op jit(solution)/shard_map/all_gather | solution.py:90
  18.1 21.6 %copy-start = (bf16[4,2,2,4,64,128]{5,4,3,2,1,0:T(8,128)(2,1)}, bf16[4,2,2,4,64,128]{5,4,3,2,1,0:T(8,128)(2,1)S(1)}, u32[]{:S(2)}) copy-start(bf16[4,2,2,4,64,128]{5,4,3,2,1,0:T(8,128)(2,1)S(1)} %maximum_bitcast_fusion.4) | copy-start | bytes 3145732
  35.2 194.6 %all-gather.8.cloned.1.call-start = ((), (), s32[]{:S(2)}) async-start(), calls=%async_computation.5 | async-start | bytes 25952256 | tf_op jit(solution)/shard_map/all_gather | solution.py:90
  46.5 1.5 slice-start.4
  48.0 18.2 %copy-start.1 = (s32[256]{0:T(256)S(1)}, s32[256]{0:T(256)}, u32[]{:S(2)}) copy-start(s32[256]{0:T(256)} %param.5) | copy-start | bytes 3076
  48.0 19.5 %copy-start.2 = (s32[256,2]{0,1:T(2,128)S(1)}, s32[256,2]{0,1:T(2,128)}, u32[]{:S(2)}) copy-start(s32[256,2]{0,1:T(2,128)} %param.4) | copy-start | bytes 6148
  62.0 165.9 %all-to-all-start = ((bf16[4,2,2,4,32,128]{5,4,3,2,1,0:T(8,128)(2,1)}), bf16[4,2,2,4,32,128]{5,4,3,2,1,0:T(8,128)(2,1)}, u32[]{:S(2)}, u32[]{:S(2)}) async-start(bf16[4,2,2,4,32,128]{5,4,3,2,1,0:T(8,128)(2,1)} %get-tuple-element.32), calls=%async_computation | async-start | bytes 1048576 | tf_op jit(solution)/shard_map/all_to_all | solution.py:78
  66.2 269.0 %all-gather.6.cloned.1.call-start = ((), (), s32[]{:S(2)}) async-start(), calls=%async_computation.4 | async-start | bytes 17301504 | tf_op jit(solution)/shard_map/all_gather | solution.py:90
  313.6 3.3 slice-start.2
  315.4 1.7 slice-start.3
  351.0 4.4 %slice-start = ((s8[6291456]{0:T(1024)(128)(4,1)}), s8[4194304]{0:T(1024)(128)(4,1)S(1)}, s32[]{:S(2)}) async-start(s8[6291456]{0:T(1024)(128)(4,1)} %bitcast.142), calls=%async_computation.6 | async-start | bytes 8388608
  352.6 2.8 slice-start.1
Sparse Core Ops, SparseCore 0:
  35.4 94.0 all-gather.3
  131.8 91.3 all-gather.7
  229.9 71.9 all-gather.5

commit v2 on v1

--- a/solution.py
+++ b/solution.py
@@ -58,7 +58,7 @@
     flat = traces.reshape(win_local * chan_local, samples)
     halves = 2
     half_bins = band_bins // halves
-    edges = [0, 3 * band_bins // 8, 6 * band_bins // 8, band_bins]
+    edges = [0, band_bins // 2, 3 * band_bins // 4, band_bins]
     spans = []
     for half in range(halves):
         ids = jnp.arange(bands * half_bins, dtype=jnp.int32)

time: 405 us -> 372 us (0.919)
  matrix products: 215 us -> 96.9 us
  waiting for transfers between devices: 61.7 us -> 142 us
    dot_general x3, matrix products: 180 us -> 56 us  [shards(): jnp.dot(picks, gathered.reshape(rows, -1), preferred_element_type=jnp.bfl...]
    all_gather x3, waiting for transfers between devices: 61.6 us -> 142 us  [shards(): gathered = lax.all_gather(piece, 'pair', axis=0, tiled=True)]
    dot_general x3, matrix products: 23.6 us -> 29.5 us  [shards(): jnp.einsum('stgkwfa,sptgkwfb->spabf', left, paired, preferred_element_typ...]
  transfers between devices with their start and end apart: 4 -> 4, of which waited for: 1 -> 3; matrix products, arithmetic and copies ran while one was open for 55% -> 30% of each run, Pallas kernels for 0% -> 0%
where the time goes in v2:
time: 372 us; the launch traced here: 365 us
  waiting for transfers between devices  142 us (38%)
  matrix products  96.9 us (26%)
  local copies, waits for them, and re-layouts  58.6 us (16%)
  blocking collectives  29 us (8%)
  other arithmetic  20.3 us (5%)
  between operations  13.7 us (4%)
  starting transfers between devices  4.39 us (1%)
    all_gather x3, waiting for transfers between devices, shards(): gathered = lax.all_gather(piece, 'pair', axis=0, tiled=True)  142 us
    dot_general x3, matrix products, shards(): jnp.dot(picks, gathered.reshape(rows, -1), preferred_element_type=jnp.bfl...  56 us
    dynamic_update_slice x3, local copies, waits for them, and re-layouts, shards(): lax.dynamic_update_slice_in_dim(out, products[part], edges[part], axis=4)  38.6 us
    dot_general x3, matrix products, shards(): jnp.einsum('stgkwfa,sptgkwfb->spabf', left, paired, preferred_element_typ...  29.5 us
    all_to_all x2, blocking collectives, shards(): lax.all_to_all(chunk_bins, 'band', split_axis=0, concat_axis=0, tiled=True)  29 us
    dot_general x2, matrix products, whiten(): lax.dot_general(dft_table(samples, bins), flat_traces, (((1,), (1,)), (()...  11.4 us
    cos x2, other arithmetic, dft_table(): jnp.cos(phase_angle)  8.42 us
  transfers between devices with their start and end apart: 4, of which 3 were waited for; matrix products, arithmetic and copies ran while one was open for 30% of the time, Pallas kernels for 0%

profile of v2, /device:TPU:1, one launch (start us, length us, event | category | flops | bytes accessed | tf_op | source)
XLA Modules:
  0.0 364.6 jit_solution(1225924862950253261)
XLA Ops:
  6.5 4.2 %fusion.58 = (f32[256,1024]{1,0:T(8,128)S(1)}, f32[256,1024]{1,0:T(8,128)S(1)}) fusion(s32[256]{0:T(256)S(1)} %fusion.68), kind=kLoop, calls=%fused_computation.85 | loop fusion | flops 3932160 | bytes 2098176 | tf_op jit(solution)/shard_map/cos | solution.py:18
  10.8 5.7 %fusion.36 = f32[512,1024]{1,0:T(8,128)S(1)} fusion(f32[1024,1024]{1,0:T(8,128)} %bitcast.140, f32[256,1024]{1,0:T(8,128)S(1)} %get-tuple-element.36, f32[256,1024]{1,0:T(8,128)S(1)} %get-tuple-element.35), kind=kOutput, calls=%fused_computation.40 | convolution fusion | flops 3221749760 | bytes 8388608 | tf_op jit(solution)/shard_map/dot_general | solution.py:24
  18.1 18.9 %all_to_all.15 = bf16[4,2,2,4,64,128]{5,4,3,2,1,0:T(8,128)(2,1)S(1)} all-to-all(bf16[4,2,2,4,64,128]{5,4,3,2,1,0:T(8,128)(2,1)S(1)} %maximum_bitcast_fusion.4), channel_id=1, replica_groups=mesh['band'=4,'pair'=32] {'band'}, dimensions={0} | all-to-all | bytes 2097152 | tf_op jit(solution)/shard_map/all_to_all | solution.py:78
  38.4 4.2 %fusion.59 = (f32[256,1024]{1,0:T(8,128)S(1)}, f32[256,1024]{1,0:T(8,128)S(1)}) fusion(s32[256]{0:T(256)S(1)} %add_add_fusion), kind=kLoop, calls=%fused_computation.86 | loop fusion | flops 3932160 | bytes 2098176 | tf_op jit(solution)/shard_map/cos | solution.py:18
  42.7 5.7 %fusion.32 = f32[512,1024]{1,0:T(8,128)S(1)} fusion(f32[1024,1024]{1,0:T(8,128)} %bitcast.141, f32[256,1024]{1,0:T(8,128)S(1)} %get-tuple-element.38, f32[256,1024]{1,0:T(8,128)S(1)} %get-tuple-element.37), kind=kOutput, calls=%fused_computation.36 | convolution fusion | flops 3221749760 | bytes 8388608 | tf_op jit(solution)/shard_map/dot_general | solution.py:24
  51.0 10.2 %all_to_all.16 = bf16[4,2,2,4,32,128]{5,4,3,2,1,0:T(8,128)(2,1)S(1)} all-to-all(bf16[4,2,2,4,32,128]{5,4,3,2,1,0:T(8,128)(2,1)S(1)} %get-tuple-element.31), channel_id=1, replica_groups=mesh['band'=4,'pair'=32] {'band'}, dimensions={0} | all-to-all | bytes 1048576 | tf_op jit(solution)/shard_map/all_to_all | solution.py:78
  62.0 3.5 all-to-all-start
  67.7 86.4 %all-gather.4.cloned.1.call-done = bf16[64,4,2,4,64,128]{5,4,3,2,1,0:T(8,128)(2,1)} async-done(((bf16[2,4,2,4,64,128]{5,4,3,2,1,0:T(8,128)(2,1)}), bf16[64,4,2,4,64,128]{5,4,3,2,1,0:T(8,128)(2,1)}) %all-gather.4.cloned.1.call-update) | async-done | bytes 33554448 | tf_op jit(solution)/shard_map/all_gather | solution.py:90
  154.1 26.2 %fusion = bf16[16,262144]{1,0:T(8,128)(2,1)S(1)} fusion(bf16[8,8,2048,128]{3,2,1,0:T(8,128)(2,1)} %bitcast.131, s32[16]{0:T(128)S(1)} %pad_add_fusion), kind=kOutput, calls=%fused_computation | convolution fusion | flops 536871936 | bytes 41943104 | tf_op jit(solution)/shard_map/dot_general | solution.py:94
  182.2 3.2 copy.64
  186.5 1.6 copy.90
  188.2 2.1 copy_negate_fusion
  190.3 3.1 maximum_bitcast_fusion
  193.4 17.0 %fusion.9 = bf16[2,2,128,128,64]{2,3,1,4,0:T(8,128)(2,1)} fusion(bf16[2,1,4,4,2,4,64,128]{7,5,2,4,3,1,6,0:T(4,128)(2,1)S(1)} %maximum_bitcast_fusion, bf16[2,1,4,4,2,4,64,128]{7,5,2,4,3,1,6,0:T(4,128)(2,1)S(1)} %copy.64, bf16[2,4,4,2,4,64,128,1]{6,5,4,3,2,1,0,7:T(8,128)(2,1)S(1)} %bitcast.142), kind=kOutput, calls=%fused_computation.10 | convolution fusion | flops 1094713344 | bytes 20971520 | tf_op jit(solution)/shard_map/stgkwfa,sptgkwfb->spabf/dot_general | solution.py:100
  211.3 17.0 %all-gather.8.cloned.1.call-done = bf16[64,4,2,4,32,128]{5,4,3,2,1,0:T(8,128)(2,1)} async-done(((bf16[2,4,2,4,32,128]{5,4,3,2,1,0:T(8,128)(2,1)}), bf16[64,4,2,4,32,128]{5,4,3,2,1,0:T(8,128)(2,1)}) %all-gather.8.cloned.1.call-update) | async-done | bytes 16777232 | tf_op jit(solution)/shard_map/all_gather | solution.py:90
  228.4 14.9 %fusion.6 = bf16[16,131072]{1,0:T(8,128)(2,1)S(1)} fusion(bf16[8,8,1024,128]{3,2,1,0:T(8,128)(2,1)} %bitcast.138, s32[16]{0:T(128)S(1)} %pad_add_fusion), kind=kOutput, calls=%fused_computation.6 | convolution fusion | flops 268436480 | bytes 20971584 | tf_op jit(solution)/shard_map/dot_general | solution.py:94
  247.0 1.4 maximum_bitcast_fusion.1
  248.4 6.3 %fusion.16 = bf16[2,2,128,128,32]{2,3,1,4,0:T(8,128)(2,1)} fusion(bf16[2,1,4,4,2,4,32,128]{7,5,2,4,3,1,6,0:T(4,128)(2,1)S(1)} %maximum_bitcast_fusion.1, bf16[2,1,4,4,2,4,32,128]{7,5,2,4,3,1,6,0:T(4,128)(2,1)S(1)} %copy.70, bf16[2,4,4,2,4,32,128,1]{6,5,4,3,2,1,0,7:T(8,128)(2,1)S(1)} %bitcast.145), kind=kOutput, calls=%fused_computation.17 | convolution fusion | flops 547356672 | bytes 10485760 | tf_op jit(solution)/shard_map/stgkwfa,sptgkwfb->spabf/dot_general | solution.py:100
  254.7 9.9 %dynamic_update_slice.9 = bf16[2,2,128,128,128]{2,3,1,4,0:T(8,128)(2,1)} pad(bf16[2,2,128,128,64]{2,3,1,4,0:T(8,128)(2,1)} %fusion.9, bf16[]{:T(256)} %constant.85.clone.1), padding=0_0x0_0x0_0x0_0x0_64 | pad | bytes 25165826 | tf_op jit(solution)/shard_map/dynamic_update_slice | solution.py:109
  264.6 38.1 %all-gather.6.cloned.1.call-done = bf16[64,4,2,4,32,128]{5,4,3,2,1,0:T(8,128)(2,1)} async-done(((bf16[2,4,2,4,32,128]{5,4,3,2,1,0:T(8,128)(2,1)}), bf16[64,4,2,4,32,128]{5,4,3,2,1,0:T(8,128)(2,1)}) %all-gather.6.cloned.1.call-update) | async-done | bytes 16777232 | tf_op jit(solution)/shard_map/all_gather | solution.py:90
  302.7 14.9 %fusion.3 = bf16[16,131072]{1,0:T(8,128)(2,1)S(1)} fusion(bf16[8,8,1024,128]{3,2,1,0:T(8,128)(2,1)} %bitcast.139, s32[16]{0:T(128)S(1)} %pad_add_fusion), kind=kOutput, calls=%fused_computation.3 | convolution fusion | flops 268436480 | bytes 20971584 | tf_op jit(solution)/shard_map/dot_general | solution.py:94
  323.0 2.8 constant_dynamic-update-slice_fusion
  325.8 6.2 %fusion.18 = bf16[2,2,128,128,128]{2,3,1,4,0:T(8,128)(2,1)} fusion(bf16[2,2,128,128,128]{2,3,1,4,0:T(8,128)(2,1)} %constant_dynamic-update-slice_fusion, bf16[2,1,4,4,2,4,32,128]{7,5,2,4,3,1,6,0:T(4,128)(2,1)S(1)} %maximum_bitcast_fusion.2, bf16[2,1,4,4,2,4,32,128]{7,5,2,4,3,1,6,0:T(4,128)(2,1)S(1)} %copy.74, ...), kind=kOutput, calls=%fused_computation.19 | convolution fusion | flops 547356672 | bytes 10485760 | tf_op jit(solution)/shard_map/stgkwfa,sptgkwfb->spabf/dot_general | solution.py:100
  332.0 25.8 %copy.76 = bf16[2,2,128,128,128]{4,3,2,1,0:T(8,128)(2,1)} copy(bf16[2,2,128,128,128]{2,3,1,4,0:T(8,128)(2,1)} %fusion.18) | data formatting | bytes 33554432 | tf_op jit(solution)/shard_map/dynamic_update_slice | solution.py:109
  (67 shorter events, 21.4 us)
Async XLA Ops:
  6.5 147.6 %all-gather.4.cloned.1.call-start = ((), (), s32[]{:S(2)}) async-start(), calls=%async_computation.3 | async-start | bytes 34603008 | tf_op jit(solution)/shard_map/all_gather | solution.py:90
  38.1 190.3 %all-gather.8.cloned.1.call-start = ((), (), s32[]{:S(2)}) async-start(), calls=%async_computation.5 | async-start | bytes 17301504 | tf_op jit(solution)/shard_map/all_gather | solution.py:90
  49.9 16.2 %copy-start.1 = (s32[256]{0:T(256)S(1)}, s32[256]{0:T(256)}, u32[]{:S(2)}) copy-start(s32[256]{0:T(256)} %param.5) | copy-start | bytes 3076
  49.9 17.4 %copy-start.2 = (s32[256,2]{0,1:T(2,128)S(1)}, s32[256,2]{0,1:T(2,128)}, u32[]{:S(2)}) copy-start(s32[256,2]{0,1:T(2,128)} %param.4) | copy-start | bytes 6148
  62.0 148.4 %all-to-all-start = ((bf16[4,2,2,4,32,128]{5,4,3,2,1,0:T(8,128)(2,1)}), bf16[4,2,2,4,32,128]{5,4,3,2,1,0:T(8,128)(2,1)S(1)}, u32[]{:S(2)}, u32[]{:S(2)}) async-start(bf16[4,2,2,4,32,128]{5,4,3,2,1,0:T(8,128)(2,1)} %get-tuple-element.32), calls=%async_computation | async-start | bytes 1048576 | tf_op jit(solution)/shard_map/all_to_all | solution.py:78
  65.5 237.2 %all-gather.6.cloned.1.call-start = ((), (), s32[]{:S(2)}) async-start(), calls=%async_computation.4 | async-start | bytes 17301504 | tf_op jit(solution)/shard_map/all_gather | solution.py:90
  320.2 2.8 copy-start
Sparse Core Ops, SparseCore 0:
  38.2 115.8 all-gather.3
  156.4 71.9 all-gather.7
  230.6 72.0 all-gather.5

commit v3 on v2

--- a/solution.py
+++ b/solution.py
@@ -58,7 +58,7 @@
     flat = traces.reshape(win_local * chan_local, samples)
     halves = 2
     half_bins = band_bins // halves
-    edges = [0, band_bins // 2, 3 * band_bins // 4, band_bins]
+    edges = [0, band_bins // 2, band_bins]
     spans = []
     for half in range(halves):
         ids = jnp.arange(bands * half_bins, dtype=jnp.int32)

time: 372 us -> 379 us (1.019)
  other arithmetic: 20.3 us -> 35.8 us
  local copies, waits for them, and re-layouts: 58.6 us -> 48.3 us
  blocking collectives: 29 us -> 34.8 us
  starting transfers between devices: 4.39 us -> 0.57 us
    dynamic_update_slice x3 -> x1, local copies, waits for them, and re-layouts: 38.6 us -> 25.8 us  [shards(): lax.dynamic_update_slice_in_dim(out, products[part], edges[part], axis=4)]
    dynamic_update_slice x0 -> x1, other arithmetic: none -> 10.6 us  [shards(): lax.dynamic_update_slice_in_dim(out, products[part], edges[part], axis=4)]
    all_to_all x2, blocking collectives: 29 us -> 34.8 us  [shards(): lax.all_to_all(chunk_bins, 'band', split_axis=0, concat_axis=0, tiled=True)]
    dot_general x3 -> x2, matrix products: 29.5 us -> 34.7 us  [shards(): jnp.einsum('stgkwfa,sptgkwfb->spabf', left, paired, preferred_element_typ...]
    another operation x3 -> x2, other arithmetic: 5.81 us -> 10 us  [shards(): paired = jnp.stack([right, rotated], axis=1)]
    dot_general x3 -> x2, matrix products: 56 us -> 52.4 us  [shards(): jnp.dot(picks, gathered.reshape(rows, -1), preferred_element_type=jnp.bfl...]
    unnamed x19 -> x17, local copies, waits for them, and re-layouts: 6.22 us -> 9.1 us
    all_gather x3 -> x2, waiting for transfers between devices: 142 us -> 140 us  [shards(): gathered = lax.all_gather(piece, 'pair', axis=0, tiled=True)]
  transfers between devices with their start and end apart: 4 -> 2, of which waited for: 3 -> 2; matrix products, arithmetic and copies ran while one was open for 30% -> 20% of each run, Pallas kernels for 0% -> 0%
where the time goes in v3:
time: 379 us; the launch traced here: 372 us
  waiting for transfers between devices  140 us (37%)
  matrix products  98.5 us (26%)
  local copies, waits for them, and re-layouts  48.3 us (13%)
  other arithmetic  35.8 us (9%)
  blocking collectives  34.8 us (9%)
  between operations  13.9 us (4%)
    all_gather x2, waiting for transfers between devices, shards(): gathered = lax.all_gather(piece, 'pair', axis=0, tiled=True)  140 us
    dot_general x2, matrix products, shards(): jnp.dot(picks, gathered.reshape(rows, -1), preferred_element_type=jnp.bfl...  52.4 us
    all_to_all x2, blocking collectives, shards(): lax.all_to_all(chunk_bins, 'band', split_axis=0, concat_axis=0, tiled=True)  34.8 us
    dot_general x2, matrix products, shards(): jnp.einsum('stgkwfa,sptgkwfb->spabf', left, paired, preferred_element_typ...  34.7 us
    dynamic_update_slice x1, local copies, waits for them, and re-layouts, shards(): lax.dynamic_update_slice_in_dim(out, products[part], edges[part], axis=4)  25.8 us
    dot_general x2, matrix products, whiten(): lax.dot_general(dft_table(samples, bins), flat_traces, (((1,), (1,)), (()...  11.5 us
    dynamic_update_slice x1, other arithmetic, shards(): lax.dynamic_update_slice_in_dim(out, products[part], edges[part], axis=4)  10.6 us
    another operation x2, other arithmetic, shards(): paired = jnp.stack([right, rotated], axis=1)  10 us
  transfers between devices with their start and end apart: 2, of which 2 were waited for; matrix products, arithmetic and copies ran while one was open for 20% of the time, Pallas kernels for 0%

profile of v3, /device:TPU:1, one launch (start us, length us, event | category | flops | bytes accessed | tf_op | source)
XLA Modules:
  0.0 372.0 jit_solution(7721512013952450237)
XLA Ops:
  6.5 4.2 %fusion.46 = (f32[256,1024]{1,0:T(8,128)S(1)}, f32[256,1024]{1,0:T(8,128)S(1)}) fusion(s32[256]{0:T(256)S(1)} %fusion.55), kind=kLoop, calls=%fused_computation.71 | loop fusion | flops 3932160 | bytes 2098176 | tf_op jit(solution)/shard_map/cos | solution.py:18
  10.8 5.7 %fusion.26 = f32[512,1024]{1,0:T(8,128)S(1)} fusion(f32[1024,1024]{1,0:T(8,128)} %bitcast.103, f32[256,1024]{1,0:T(8,128)S(1)} %get-tuple-element.26, f32[256,1024]{1,0:T(8,128)S(1)} %get-tuple-element.25), kind=kOutput, calls=%fused_computation.31 | convolution fusion | flops 3221749760 | bytes 8388608 | tf_op jit(solution)/shard_map/dot_general | solution.py:24
  18.1 18.9 %all_to_all.10 = bf16[4,2,2,4,64,128]{5,4,3,2,1,0:T(8,128)(2,1)S(1)} all-to-all(bf16[4,2,2,4,64,128]{5,4,3,2,1,0:T(8,128)(2,1)S(1)} %maximum_bitcast_fusion.3), channel_id=1, replica_groups=mesh['band'=4,'pair'=32] {'band'}, dimensions={0} | all-to-all | bytes 2097152 | tf_op jit(solution)/shard_map/all_to_all | solution.py:78
  38.7 4.2 %fusion.47 = (f32[256,1024]{1,0:T(8,128)S(1)}, f32[256,1024]{1,0:T(8,128)S(1)}) fusion(s32[256]{0:T(256)S(1)} %add_add_fusion), kind=kLoop, calls=%fused_computation.72 | loop fusion | flops 3932160 | bytes 2098176 | tf_op jit(solution)/shard_map/cos | solution.py:18
  42.9 5.7 %fusion.22 = f32[512,1024]{1,0:T(8,128)S(1)} fusion(f32[1024,1024]{1,0:T(8,128)} %bitcast.104, f32[256,1024]{1,0:T(8,128)S(1)} %get-tuple-element.28, f32[256,1024]{1,0:T(8,128)S(1)} %get-tuple-element.27), kind=kOutput, calls=%fused_computation.27 | convolution fusion | flops 3221749760 | bytes 8388608 | tf_op jit(solution)/shard_map/dot_general | solution.py:24
  50.3 16.0 %all_to_all.11 = bf16[4,2,2,4,64,128]{5,4,3,2,1,0:T(8,128)(2,1)S(1)} all-to-all(bf16[4,2,2,4,64,128]{5,4,3,2,1,0:T(8,128)(2,1)S(1)} %maximum_bitcast_fusion.2), channel_id=1, replica_groups=mesh['band'=4,'pair'=32] {'band'}, dimensions={0} | all-to-all | bytes 2097152 | tf_op jit(solution)/shard_map/all_to_all | solution.py:78
  69.0 85.1 %all-gather.5.cloned.1.call-done = bf16[64,4,2,4,64,128]{5,4,3,2,1,0:T(8,128)(2,1)} async-done(((bf16[2,4,2,4,64,128]{5,4,3,2,1,0:T(8,128)(2,1)}), bf16[64,4,2,4,64,128]{5,4,3,2,1,0:T(8,128)(2,1)}) %all-gather.5.cloned.1.call-update) | async-done | bytes 33554448 | tf_op jit(solution)/shard_map/all_gather | solution.py:90
  154.1 26.2 %fusion.3 = bf16[16,262144]{1,0:T(8,128)(2,1)S(1)} fusion(bf16[8,8,2048,128]{3,2,1,0:T(8,128)(2,1)} %bitcast.97, s32[16]{0:T(128)S(1)} %pad_add_fusion), kind=kOutput, calls=%fused_computation.3 | convolution fusion | flops 536871936 | bytes 41943104 | tf_op jit(solution)/shard_map/dot_general | solution.py:94
  181.7 1.4 fusion.61
  183.1 1.6 copy.68
  184.7 3.2 copy.52
  188.5 2.1 copy_negate_fusion.1
  190.7 5.2 %maximum_bitcast_fusion = bf16[2,1,4,4,2,4,64,128]{7,5,2,4,3,1,6,0:T(4,128)(2,1)} fusion(bf16[2,4,4,1,4,64,128]{6,4,1,3,2,5,0:T(4,128)(2,1)S(1)} %copy.68, bf16[2,4,4,1,4,64,128]{6,4,1,3,2,5,0:T(4,128)(2,1)S(1)} %copy_negate_fusion.1), kind=kLoop, calls=%fused_computation.23 | loop fusion | flops 2097152 | bytes 8388608 | tf_op jit(solution)/shard_map/stack | solution.py:99
  195.8 18.7 %fusion.6 = bf16[2,2,128,128,64]{2,3,1,4,0:T(8,128)(2,1)} fusion(bf16[2,1,4,4,2,4,64,128]{7,5,2,4,3,1,6,0:T(4,128)(2,1)} %maximum_bitcast_fusion, bf16[2,1,4,4,2,4,64,128]{7,5,2,4,3,1,6,0:T(4,128)(2,1)S(1)} %copy.52, bf16[2,4,4,2,4,64,128,1]{6,5,4,3,2,1,0,7:T(8,128)(2,1)S(1)} %bitcast.107), kind=kOutput, calls=%fused_computation.9 | convolution fusion | flops 1094713344 | bytes 20971520 | tf_op jit(solution)/shard_map/stgkwfa,sptgkwfb->spabf/dot_general | solution.py:100
  214.6 54.9 %all-gather.3.cloned.1.call-done = bf16[64,4,2,4,64,128]{5,4,3,2,1,0:T(8,128)(2,1)} async-done(((bf16[2,4,2,4,64,128]{5,4,3,2,1,0:T(8,128)(2,1)}), bf16[64,4,2,4,64,128]{5,4,3,2,1,0:T(8,128)(2,1)}) %all-gather.3.cloned.1.call-update) | async-done | bytes 33554448 | tf_op jit(solution)/shard_map/all_gather | solution.py:90
  269.5 26.2 %fusion = bf16[16,262144]{1,0:T(8,128)(2,1)S(1)} fusion(bf16[8,8,2048,128]{3,2,1,0:T(8,128)(2,1)} %bitcast.98, s32[16]{0:T(128)S(1)} %pad_add_fusion), kind=kOutput, calls=%fused_computation | convolution fusion | flops 536871936 | bytes 41943104 | tf_op jit(solution)/shard_map/dot_general | solution.py:94
  298.1 1.6 copy.70
  299.7 2.1 copy_negate_fusion
  301.8 3.2 copy.56
  305.1 2.6 copy.79
  307.7 4.8 %maximum_bitcast_fusion.1 = bf16[2,1,4,4,2,4,64,128]{7,5,2,4,3,1,6,0:T(4,128)(2,1)} fusion(bf16[2,4,4,1,4,64,128]{6,4,1,3,2,5,0:T(4,128)(2,1)S(1)} %copy.70, bf16[2,4,4,1,4,64,128]{6,4,1,3,2,5,0:T(4,128)(2,1)S(1)} %copy_negate_fusion), kind=kLoop, calls=%fused_computation.24 | loop fusion | flops 2097152 | bytes 8388608 | tf_op jit(solution)/shard_map/stack | solution.py:99
  312.5 15.9 %fusion.7 = bf16[2,2,128,128,64]{2,3,1,4,0:T(8,128)(2,1)} fusion(bf16[2,1,4,4,2,4,64,128]{7,5,2,4,3,1,6,0:T(4,128)(2,1)} %maximum_bitcast_fusion.1, bf16[2,1,4,4,2,4,64,128]{7,5,2,4,3,1,6,0:T(4,128)(2,1)S(1)} %copy.56, bf16[2,4,4,2,4,64,128,1]{6,5,4,3,2,1,0,7:T(8,128)(2,1)} %bitcast.108), kind=kOutput, calls=%fused_computation.10 | convolution fusion | flops 1094713344 | bytes 20971520 | tf_op jit(solution)/shard_map/stgkwfa,sptgkwfb->spabf/dot_general | solution.py:100
  328.5 10.6 %pad_maximum_fusion = bf16[2,2,128,128,128]{2,3,1,4,0:T(8,128)(2,1)} fusion(bf16[2,2,128,128,64]{2,3,1,4,0:T(8,128)(2,1)} %fusion.7, bf16[2,2,128,128,64]{2,3,1,4,0:T(8,128)(2,1)S(1)} %bitcast.106), kind=kLoop, calls=%fused_computation.6 | loop fusion | flops 8388608 | bytes 33554432 | tf_op jit(solution)/shard_map/dynamic_update_slice | solution.py:109
  339.1 25.8 %copy.58 = bf16[2,2,128,128,128]{4,3,2,1,0:T(8,128)(2,1)} copy(bf16[2,2,128,128,128]{2,3,1,4,0:T(8,128)(2,1)} %pad_maximum_fusion) | data formatting | bytes 33554432 | tf_op jit(solution)/shard_map/dynamic_update_slice | solution.py:109
  (52 shorter events, 11.8 us)
Async XLA Ops:
  6.5 147.6 %all-gather.5.cloned.1.call-start = ((), (), s32[]{:S(2)}) async-start(), calls=%async_computation.3 | async-start | bytes 34603008 | tf_op jit(solution)/shard_map/all_gather | solution.py:90
  38.1 231.4 %all-gather.3.cloned.1.call-start = ((), (), s32[]{:S(2)}) async-start(), calls=%async_computation.2 | async-start | bytes 34603008 | tf_op jit(solution)/shard_map/all_gather | solution.py:90
  50.0 17.3 %copy-start = (s32[256]{0:T(256)S(1)}, s32[256]{0:T(256)}, u32[]{:S(2)}) copy-start(s32[256]{0:T(256)} %param.5) | copy-start | bytes 3076
  50.0 18.6 %copy-start.1 = (s32[256,2]{0,1:T(2,128)S(1)}, s32[256,2]{0,1:T(2,128)}, u32[]{:S(2)}) copy-start(s32[256,2]{0,1:T(2,128)} %param.4) | copy-start | bytes 6148
  307.7 20.8 %slice-start = ((s8[8388608]{0:T(1024)(128)(4,1)}), s8[4194304]{0:T(1024)(128)(4,1)S(1)}, s32[]{:S(2)}) async-start(s8[8388608]{0:T(1024)(128)(4,1)} %bitcast.105), calls=%async_computation.4 | async-start | bytes 8388608
  312.5 15.9 %slice-start.1 = ((s8[8388608]{0:T(1024)(128)(4,1)}), s8[4194304]{0:T(1024)(128)(4,1)S(1)}, s32[]{:S(2)}) async-start(s8[8388608]{0:T(1024)(128)(4,1)} %bitcast.105), calls=%async_computation.5 | async-start | bytes 8388608
Sparse Core Ops, SparseCore 0:
  38.2 115.8 all-gather.4
  156.4 113.0 all-gather.2

commit v4 on v2

--- a/solution.py
+++ b/solution.py
@@ -1,3 +1,4 @@
+import numpy as np
 import jax
 import jax.numpy as jnp
 from jax import lax
@@ -12,10 +13,8 @@
 
 
 def dft_table(samples, bins):
-    bin_ids = jnp.broadcast_to(bins[:, None], (bins.shape[0], samples))
-    sample_ids = lax.broadcasted_iota(jnp.int32, (bins.shape[0], samples), 1)
-    phase_angle = (sample_ids * bin_ids % samples).astype(jnp.float32) * (2.0 * jnp.pi / samples)
-    return jnp.concatenate([jnp.cos(phase_angle), -jnp.sin(phase_angle)], axis=0)
+    phase_angle = (np.arange(samples)[None, :] * bins[:, None] % samples) * (2.0 * np.pi / samples)
+    return jnp.asarray(np.concatenate([np.cos(phase_angle), -np.sin(phase_angle)], axis=0).astype(np.float32))
 
 
 def whiten(flat_traces, bins):
@@ -61,7 +60,7 @@
     edges = [0, band_bins // 2, 3 * band_bins // 4, band_bins]
     spans = []
     for half in range(halves):
-        ids = jnp.arange(bands * half_bins, dtype=jnp.int32)
+        ids = np.arange(bands * half_bins)
         bins = (ids // half_bins) * band_bins + half * half_bins + ids % half_bins
         whitened = whiten(flat, bins)
         whitened = whitened.reshape(2, bands, half_bins, win_local, per_device, BLOCK)

time: 372 us -> 368 us (0.989)
  other arithmetic: 20.3 us -> 11.6 us
  waiting for transfers between devices: 142 us -> 146 us
    cos x2 -> x0, other arithmetic: 8.42 us -> none  [dft_table(): jnp.cos(phase_angle)]
    all_gather x3, waiting for transfers between devices: 142 us -> 146 us  [shards(): gathered = lax.all_gather(piece, 'pair', axis=0, tiled=True)]
  transfers between devices with their start and end apart: 4 -> 4, of which waited for: 3 -> 3; matrix products, arithmetic and copies ran while one was open for 30% -> 29% of each run, Pallas kernels for 0% -> 0%
where the time goes in v4:
time: 368 us; the launch traced here: 361 us
  waiting for transfers between devices  146 us (40%)
  matrix products  97.5 us (26%)
  local copies, waits for them, and re-layouts  59.3 us (16%)
  blocking collectives  29.1 us (8%)
  between operations  13.7 us (4%)
  other arithmetic  11.6 us (3%)
  starting transfers between devices  3.87 us (1%)
    all_gather x3, waiting for transfers between devices, shards(): gathered = lax.all_gather(piece, 'pair', axis=0, tiled=True)  146 us
    dot_general x3, matrix products, shards(): jnp.dot(picks, gathered.reshape(rows, -1), preferred_element_type=jnp.bfl...  56 us
    dynamic_update_slice x3, local copies, waits for them, and re-layouts, shards(): lax.dynamic_update_slice_in_dim(out, products[part], edges[part], axis=4)  38.7 us
    dot_general x3, matrix products, shards(): jnp.einsum('stgkwfa,sptgkwfb->spabf', left, paired, preferred_element_typ...  29.5 us
    all_to_all x2, blocking collectives, shards(): lax.all_to_all(chunk_bins, 'band', split_axis=0, concat_axis=0, tiled=True)  29.1 us
    dot_general x2, matrix products, whiten(): lax.dot_general(dft_table(samples, bins), flat_traces, (((1,), (1,)), (()...  12 us
  transfers between devices with their start and end apart: 4, of which 3 were waited for; matrix products, arithmetic and copies ran while one was open for 29% of the time, Pallas kernels for 0%

profile of v4, /device:TPU:1, one launch (start us, length us, event | category | flops | bytes accessed | tf_op | source)
XLA Modules:
  0.0 361.0 jit_solution(15198788224465309761)
XLA Ops:
  6.5 6.3 %fusion.52 = f32[512,1024]{1,0:T(8,128)S(1)} fusion(f32[512,1024]{1,0:T(8,128)} %constant.33.clone, f32[1024,1024]{1,0:T(8,128)} %bitcast.142), kind=kOutput, calls=%fused_computation.85 | convolution fusion | flops 3221225472 | bytes 8388608 | tf_op jit(solution)/shard_map/dot_general | solution.py:23
  14.5 19.0 %all_to_all.15 = bf16[4,2,2,4,64,128]{5,4,3,2,1,0:T(8,128)(2,1)S(1)} all-to-all(bf16[4,2,2,4,64,128]{5,4,3,2,1,0:T(8,128)(2,1)S(1)} %maximum_bitcast_fusion.4), channel_id=1, replica_groups=mesh['band'=4,'pair'=32] {'band'}, dimensions={0} | all-to-all | bytes 2097152 | tf_op jit(solution)/shard_map/all_to_all | solution.py:77
  34.7 5.7 %fusion.51 = f32[512,1024]{1,0:T(8,128)S(1)} fusion(f32[512,1024]{1,0:T(8,128)S(1)} %copy-done.1, f32[1024,1024]{1,0:T(8,128)} %bitcast.143), kind=kOutput, calls=%fused_computation.84 | convolution fusion | flops 3221225472 | bytes 8388608 | tf_op jit(solution)/shard_map/dot_general | solution.py:23
  42.9 10.1 %all_to_all.16 = bf16[4,2,2,4,32,128]{5,4,3,2,1,0:T(8,128)(2,1)S(1)} all-to-all(bf16[4,2,2,4,32,128]{5,4,3,2,1,0:T(8,128)(2,1)S(1)} %get-tuple-element.31), channel_id=1, replica_groups=mesh['band'=4,'pair'=32] {'band'}, dimensions={0} | all-to-all | bytes 1048576 | tf_op jit(solution)/shard_map/all_to_all | solution.py:77
  54.0 3.5 all-to-all-start
  59.5 91.2 %all-gather.4.cloned.1.call-done = bf16[64,4,2,4,64,128]{5,4,3,2,1,0:T(8,128)(2,1)} async-done(((bf16[2,4,2,4,64,128]{5,4,3,2,1,0:T(8,128)(2,1)}), bf16[64,4,2,4,64,128]{5,4,3,2,1,0:T(8,128)(2,1)}) %all-gather.4.cloned.1.call-update) | async-done | bytes 33554448 | tf_op jit(solution)/shard_map/all_gather | solution.py:89
  150.7 26.2 %fusion = bf16[16,262144]{1,0:T(8,128)(2,1)S(1)} fusion(bf16[8,8,2048,128]{3,2,1,0:T(8,128)(2,1)} %bitcast.133, s32[16]{0:T(128)S(1)} %pad_add_fusion), kind=kOutput, calls=%fused_computation | convolution fusion | flops 536871936 | bytes 41943104 | tf_op jit(solution)/shard_map/dot_general | solution.py:93
  176.8 1.2 slice_bitcast_fusion
  179.1 3.2 copy.66
  183.4 1.6 copy.92
  185.1 2.1 copy_negate_fusion
  187.2 2.9 maximum_bitcast_fusion
  190.1 17.0 %fusion.9 = bf16[2,2,128,128,64]{2,3,1,4,0:T(8,128)(2,1)} fusion(bf16[2,1,4,4,2,4,64,128]{7,5,2,4,3,1,6,0:T(4,128)(2,1)S(1)} %maximum_bitcast_fusion, bf16[2,1,4,4,2,4,64,128]{7,5,2,4,3,1,6,0:T(4,128)(2,1)S(1)} %copy.66, bf16[2,4,4,2,4,64,128,1]{6,5,4,3,2,1,0,7:T(8,128)(2,1)S(1)} %bitcast.144), kind=kOutput, calls=%fused_computation.10 | convolution fusion | flops 1094713344 | bytes 20971520 | tf_op jit(solution)/shard_map/stgkwfa,sptgkwfb->spabf/dot_general | solution.py:99
  208.0 16.9 %all-gather.8.cloned.1.call-done = bf16[64,4,2,4,32,128]{5,4,3,2,1,0:T(8,128)(2,1)} async-done(((bf16[2,4,2,4,32,128]{5,4,3,2,1,0:T(8,128)(2,1)}), bf16[64,4,2,4,32,128]{5,4,3,2,1,0:T(8,128)(2,1)}) %all-gather.8.cloned.1.call-update) | async-done | bytes 16777232 | tf_op jit(solution)/shard_map/all_gather | solution.py:89
  224.9 14.9 %fusion.6 = bf16[16,131072]{1,0:T(8,128)(2,1)S(1)} fusion(bf16[8,8,1024,128]{3,2,1,0:T(8,128)(2,1)} %bitcast.140, s32[16]{0:T(128)S(1)} %pad_add_fusion), kind=kOutput, calls=%fused_computation.6 | convolution fusion | flops 268436480 | bytes 20971584 | tf_op jit(solution)/shard_map/dot_general | solution.py:93
  243.8 1.4 maximum_bitcast_fusion.1
  245.1 6.3 %fusion.16 = bf16[2,2,128,128,32]{2,3,1,4,0:T(8,128)(2,1)} fusion(bf16[2,1,4,4,2,4,32,128]{7,5,2,4,3,1,6,0:T(4,128)(2,1)S(1)} %maximum_bitcast_fusion.1, bf16[2,1,4,4,2,4,32,128]{7,5,2,4,3,1,6,0:T(4,128)(2,1)S(1)} %copy.72, bf16[2,4,4,2,4,32,128,1]{6,5,4,3,2,1,0,7:T(8,128)(2,1)S(1)} %bitcast.147), kind=kOutput, calls=%fused_computation.17 | convolution fusion | flops 547356672 | bytes 10485760 | tf_op jit(solution)/shard_map/stgkwfa,sptgkwfb->spabf/dot_general | solution.py:99
  251.4 10.0 %dynamic_update_slice.9 = bf16[2,2,128,128,128]{2,3,1,4,0:T(8,128)(2,1)} pad(bf16[2,2,128,128,64]{2,3,1,4,0:T(8,128)(2,1)} %fusion.9, bf16[]{:T(256)} %constant.30.clone.1), padding=0_0x0_0x0_0x0_0x0_64 | pad | bytes 25165826 | tf_op jit(solution)/shard_map/dynamic_update_slice | solution.py:108
  261.4 37.8 %all-gather.6.cloned.1.call-done = bf16[64,4,2,4,32,128]{5,4,3,2,1,0:T(8,128)(2,1)} async-done(((bf16[2,4,2,4,32,128]{5,4,3,2,1,0:T(8,128)(2,1)}), bf16[64,4,2,4,32,128]{5,4,3,2,1,0:T(8,128)(2,1)}) %all-gather.6.cloned.1.call-update) | async-done | bytes 16777232 | tf_op jit(solution)/shard_map/all_gather | solution.py:89
  299.3 14.9 %fusion.3 = bf16[16,131072]{1,0:T(8,128)(2,1)S(1)} fusion(bf16[8,8,1024,128]{3,2,1,0:T(8,128)(2,1)} %bitcast.141, s32[16]{0:T(128)S(1)} %pad_add_fusion), kind=kOutput, calls=%fused_computation.3 | convolution fusion | flops 268436480 | bytes 20971584 | tf_op jit(solution)/shard_map/dot_general | solution.py:93
  318.1 1.4 maximum_bitcast_fusion.2
  319.5 2.8 constant_dynamic-update-slice_fusion
  322.3 6.2 %fusion.18 = bf16[2,2,128,128,128]{2,3,1,4,0:T(8,128)(2,1)} fusion(bf16[2,2,128,128,128]{2,3,1,4,0:T(8,128)(2,1)} %constant_dynamic-update-slice_fusion, bf16[2,1,4,4,2,4,32,128]{7,5,2,4,3,1,6,0:T(4,128)(2,1)S(1)} %maximum_bitcast_fusion.2, bf16[2,1,4,4,2,4,32,128]{7,5,2,4,3,1,6,0:T(4,128)(2,1)S(1)} %copy.76, ...), kind=kOutput, calls=%fused_computation.19 | convolution fusion | flops 547356672 | bytes 10485760 | tf_op jit(solution)/shard_map/stgkwfa,sptgkwfb->spabf/dot_general | solution.py:99
  328.5 25.8 %copy.78 = bf16[2,2,128,128,128]{4,3,2,1,0:T(8,128)(2,1)} copy(bf16[2,2,128,128,128]{2,3,1,4,0:T(8,128)(2,1)} %fusion.18) | data formatting | bytes 33554432 | tf_op jit(solution)/shard_map/dynamic_update_slice | solution.py:108
  (65 shorter events, 18.9 us)
Async XLA Ops:
  6.5 144.1 %all-gather.4.cloned.1.call-start = ((), (), s32[]{:S(2)}) async-start(), calls=%async_computation.3 | async-start | bytes 34603008 | tf_op jit(solution)/shard_map/all_gather | solution.py:89
  14.5 20.1 %copy-start.1 = (f32[512,1024]{1,0:T(8,128)S(1)}, f32[512,1024]{1,0:T(8,128)}, u32[]{:S(2)}) copy-start(f32[512,1024]{1,0:T(8,128)} %constant.34.clone) | copy-start | bytes 6291460
  34.6 190.3 %all-gather.8.cloned.1.call-start = ((), (), s32[]{:S(2)}) async-start(), calls=%async_computation.5 | async-start | bytes 17301504 | tf_op jit(solution)/shard_map/all_gather | solution.py:89
  41.9 15.9 %copy-start.2 = (s32[256]{0:T(256)S(1)}, s32[256]{0:T(256)}, u32[]{:S(2)}) copy-start(s32[256]{0:T(256)} %param.7) | copy-start | bytes 3076
  41.9 17.2 %copy-start.3 = (s32[256,2]{0,1:T(2,128)S(1)}, s32[256,2]{0,1:T(2,128)}, u32[]{:S(2)}) copy-start(s32[256,2]{0,1:T(2,128)} %param.6) | copy-start | bytes 6148
  54.0 153.2 %all-to-all-start = ((bf16[4,2,2,4,32,128]{5,4,3,2,1,0:T(8,128)(2,1)}), bf16[4,2,2,4,32,128]{5,4,3,2,1,0:T(8,128)(2,1)S(1)}, u32[]{:S(2)}, u32[]{:S(2)}) async-start(bf16[4,2,2,4,32,128]{5,4,3,2,1,0:T(8,128)(2,1)} %get-tuple-element.32), calls=%async_computation | async-start | bytes 1048576 | tf_op jit(solution)/shard_map/all_to_all | solution.py:77
  57.4 241.8 %all-gather.6.cloned.1.call-start = ((), (), s32[]{:S(2)}) async-start(), calls=%async_computation.4 | async-start | bytes 17301504 | tf_op jit(solution)/shard_map/all_gather | solution.py:89
  316.8 2.7 copy-start
Sparse Core Ops, SparseCore 0:
  34.7 115.8 all-gather.3
  152.9 71.9 all-gather.7
  227.1 72.0 all-gather.5
